TPU v7x, 256 devices: a whole 4x4x8 slice. The times are simulated.
256 devices in a mesh: ctx: 64 (over x_hi, z, y), head: 4 (over x_lo, core).
Axes of the slice: x: 4 (x_hi: 2, x_lo: 2; x = x_hi * 2 + x_lo), y: 4, z: 8, core: 2. Of those that a mesh axis runs over, the one named last changes fastest.
Arguments:
- queries: bfloat16 [8192, 16, 128], P('ctx', 'head'), may hold values from -30 to 30
- rotated_keys: bfloat16 [8192, 8, 128], P('ctx', 'head'), may hold values from -4 to 4
- value_vectors: bfloat16 [8192, 8, 128], P('ctx', 'head'), may hold values from -6 to 6
- out_grad: bfloat16 [8192, 5376], P('ctx', 'head'), may hold values from -16 to 16
- out_proj: bfloat16 [5376, 2048], P('ctx', 'head'), may hold values from -0.125 to 0.125
- seg_ids: int32 [8192], replicated, may hold values from 0 to 15, never falling along the last dimension, each value on 1 to 4096 neighbouring positions
Outputs:
- layer_out: bfloat16 [8192, 5376], P('ctx', 'head')
- query_gradient: bfloat16 [8192, 16, 128], P('ctx', 'head')
- grad_key: bfloat16 [8192, 8, 128], P('ctx', 'head')
- grad_value: bfloat16 [8192, 8, 128], P('ctx', 'head')
- grad_proj: float32 [5376, 2048], P('ctx', 'head')
Inputs may be any that keep to these rules, and one draw needn't show every extreme that they name: `seg_ids`: segment ids never fall along the slab; every one of the 16 books holds one token or more.
All inputs are finite; a program needn't handle non-finite values.
Results may differ from a plain program's by a relative error of at most 0.025.
Values may be sent and summed in bfloat16 or wider, within the bound.
No kernel may reach another device: no remote copies, remote signals or barrier semaphores. Data moves between devices by JAX's collectives and lax.ppermute only.
A program may use at most 128 MiB of HBM per device.

v0:
```python
import jax
import jax.numpy as jnp
from jax import lax
from jax.sharding import PartitionSpec as P

WINDOW_TOKENS = 1024


def passed_along(value, axis, by):
    count = lax.axis_size(axis)
    pairs = [(i, i + by) for i in range(count) if 0 <= i + by < count]
    return lax.ppermute(value, axis, pairs)


def shards(queries, rotated_keys, value_vectors, out_grad, out_proj, seg_ids):
    logit_scale = 168.0 ** (-0.5)
    tok_rows = queries.shape[0]
    heads_query = queries.shape[1]
    heads_kv = rotated_keys.shape[1]
    head_size = queries.shape[2]
    group_size = heads_query // heads_kv
    blocks = WINDOW_TOKENS // tok_rows
    ctx_count = lax.axis_size("ctx")
    ctx_index = lax.axis_index("ctx")
    own_block = jnp.stack([rotated_keys, value_vectors])
    received = []
    for offset in range(blocks):
        received.append(passed_along(own_block, "ctx", offset + 1))
    key_value = jnp.concatenate(received[::-1] + [own_block], axis=1)
    key_row_slice = key_value[0]
    value_row_slice = key_value[1]
    first_row = ctx_index * tok_rows
    seg_padded = jnp.concatenate([jnp.full((WINDOW_TOKENS,), -1, jnp.int32), seg_ids], 0)
    key_seg = lax.dynamic_slice_in_dim(seg_padded, first_row, WINDOW_TOKENS + tok_rows, 0)
    query_seg = lax.dynamic_slice_in_dim(seg_ids, first_row, tok_rows, 0)
    query_pos = first_row + jnp.arange(tok_rows, dtype=jnp.int32)
    key_pos = first_row - WINDOW_TOKENS + jnp.arange(WINDOW_TOKENS + tok_rows, dtype=jnp.int32)
    allowed = (key_pos[None, :] <= query_pos[:, None]) & (
        query_pos[:, None] - key_pos[None, :] < WINDOW_TOKENS
    )
    allowed = allowed & (key_pos[None, :] >= 0) & (query_seg[:, None] == key_seg[None, :])
    grouped_queries = queries.reshape(tok_rows, heads_kv, group_size, head_size)
    attention_logits = logit_scale * jnp.einsum(
        "eqco,fqo->qcef", grouped_queries, key_row_slice, preferred_element_type=jnp.float32
    )
    attention_logits = jnp.where(allowed, attention_logits, -1e30)
    top_score = jnp.max(attention_logits, axis=3, keepdims=True)
    weights = jnp.where(allowed, jnp.exp(attention_logits - top_score), 0.0)
    probs = weights / jnp.sum(weights, axis=3, keepdims=True)
    probabilities_half = probs.astype(jnp.bfloat16)
    attended_output = jnp.einsum(
        "ykip,pyj->iykj", probabilities_half, value_row_slice, preferred_element_type=jnp.float32
    )
    attended_output = attended_output.astype(jnp.bfloat16).reshape(
        tok_rows, heads_query * head_size
    )
    proj_full = lax.all_gather(out_proj, "ctx", axis=0, tiled=True)
    out_partial = lax.dot_general(
        attended_output, proj_full, (((1,), (1,)), ((), ())), preferred_element_type=jnp.float32
    )
    layer_out = lax.psum_scatter(out_partial, "head", scatter_dimension=1, tiled=True).astype(
        jnp.bfloat16
    )
    grad_full = lax.all_gather(out_grad, "head", axis=1, tiled=True)
    grad_attended = jnp.dot(grad_full, proj_full, preferred_element_type=jnp.float32).astype(
        jnp.bfloat16
    )
    proj_rows = grad_full.shape[1] // ctx_count
    proj_partial = jnp.einsum(
        "tcr,tj->crj",
        grad_full.reshape(tok_rows, ctx_count, proj_rows),
        attended_output,
        preferred_element_type=jnp.float32,
    )
    proj_summed = lax.psum_scatter(proj_partial, "ctx", scatter_dimension=0, tiled=True)
    grad_proj = proj_summed.reshape(proj_rows, -1) * (ctx_count * tok_rows) ** (-0.5)
    grouped_gradient = grad_attended.reshape(tok_rows, heads_kv, group_size, head_size)
    attn_groups = attended_output.reshape(tok_rows, heads_kv, group_size, head_size)
    probability_gradient = jnp.einsum(
        "eqco,fqo->qcef", grouped_gradient, value_row_slice, preferred_element_type=jnp.float32
    )
    row_delta = jnp.sum(
        grouped_gradient.astype(jnp.float32) * attn_groups.astype(jnp.float32), axis=3
    )
    row_delta = jnp.transpose(row_delta, (1, 2, 0))[..., None]
    score_gradient = (probs * (probability_gradient - row_delta)).astype(jnp.bfloat16)
    query_gradient = logit_scale * jnp.einsum(
        "ykip,pyj->iykj", score_gradient, key_row_slice, preferred_element_type=jnp.float32
    )
    query_gradient = query_gradient.astype(jnp.bfloat16).reshape(tok_rows, heads_query, head_size)
    key_portion = logit_scale * jnp.einsum(
        "huoe,ohul->ehl", score_gradient, grouped_queries, preferred_element_type=jnp.float32
    )
    value_portion = jnp.einsum(
        "huoe,ohul->ehl", probabilities_half, grouped_gradient, preferred_element_type=jnp.float32
    )
    both_parts = jnp.stack([key_portion, value_portion])
    halo_part = both_parts[:, :WINDOW_TOKENS]
    summed = both_parts[:, WINDOW_TOKENS:]
    for offset in range(blocks):
        distance = offset + 1
        portion = halo_part[:, (blocks - distance) * tok_rows : (blocks - distance + 1) * tok_rows]
        summed = summed + passed_along(portion, "ctx", -distance)
    grad_key = summed[0].astype(jnp.bfloat16)
    grad_value = summed[1].astype(jnp.bfloat16)
    return (layer_out, query_gradient, grad_key, grad_value, grad_proj)


def solution(mesh):
    return jax.shard_map(
        shards,
        mesh=mesh,
        in_specs=(
            P("ctx", "head", None),
            P("ctx", "head", None),
            P("ctx", "head", None),
            P("ctx", "head"),
            P("ctx", "head"),
            P(),
        ),
        out_specs=(
            P("ctx", "head"),
            P("ctx", "head", None),
            P("ctx", "head", None),
            P("ctx", "head", None),
            P("ctx", "head"),
        ),
        check_vma=False,
    )
```

profile of v0, /device:TPU:6, one launch (start us, length us, event | category | flops | bytes accessed | tf_op | source)
XLA Modules:
  0.0 658.0 jit_solution(7047656950511083596)
XLA Ops:
  8.9 3.5 collective-permute-start.7
  12.4 4.8 collective-permute-start.6
  17.2 4.6 collective-permute-start.5
  21.8 4.5 collective-permute-start.1
  26.3 5.5 collective-permute-start
  34.5 5.3 collective-permute-done
  39.7 8.6 %collective-permute-start.2 = (bf16[2,128,2,128]{3,1,2,0:T(8,128)(2,1)S(1)}, bf16[2,128,2,128]{3,1,2,0:T(8,128)(2,1)S(1)}, u32[]{:S(2)}, u32[]{:S(2)}) collective-permute-start(bf16[2,128,2,128]{3,1,2,0:T(8,128)(2,1)S(1)} %pad_maximum_fusion.1), channel_id=1, source_target_pairs={{0,24},{4,28},{8,32},{12,36},{16,40},{20,44},{24,48},{28,52},{32,5... | collective-permute-start | bytes 393224 | tf_op jit(solution)/shard_map/ppermute | solution.py:12
  50.3 4.2 collective-permute-done.2
  54.5 6.3 collective-permute-start.4
  69.4 79.3 %all-gather.6.cloned.1.call-done = bf16[64,84,512]{2,1,0:T(8,128)(2,1)} async-done(((bf16[1,84,512]{2,1,0:T(8,128)(2,1)}), bf16[64,84,512]{2,1,0:T(8,128)(2,1)}) %all-gather.6.cloned.1.call-update) | async-done | bytes 5505040 | tf_op jit(solution)/shard_map/all_gather | solution.py:57
  148.7 8.9 %reshape.53 = bf16[5376,512]{1,0:T(8,128)(2,1)} reshape(bf16[64,84,512]{2,1,0:T(8,128)(2,1)} %all-gather.6.cloned.1.call-done) | data formatting | bytes 11010048
  157.6 16.0 %all-gather.4.cloned.1.call-done = bf16[128,5376]{0,1:T(8,128)(2,1)} async-done(((bf16[128,1344]{0,1:T(8,128)(2,1)}), bf16[128,5376]{0,1:T(8,128)(2,1)}) %all-gather.4.cloned.1.call-update) | async-done | bytes 1376272 | tf_op jit(solution)/shard_map/all_gather | solution.py:64
  173.6 3.9 convolution_convert_fusion
  178.0 5.8 fusion.45
  186.1 6.0 convolution_bitcast_fusion
  197.8 8.3 %collective-permute-start.8 = (f32[2,128,2,128]{3,1,2,0:T(8,128)S(1)}, f32[2,128,2,128]{3,1,2,0:T(8,128)S(1)}, u32[]{:S(2)}, u32[]{:S(2)}) collective-permute-start(f32[2,128,2,128]{3,1,2,0:T(8,128)S(1)} %get-tuple-element.20), channel_id=1, source_target_pairs={{4,0},{8,4},{12,8},{16,12},{20,16},{24,20},{28,24},{32,28},{36,32}... | collective-permute-start | bytes 786440 | tf_op jit(solution)/shard_map/ppermute | solution.py:12
  208.9 3.6 collective-permute-start.10
  215.8 5.1 collective-permute-start.12
  227.5 5.3 collective-permute-start.14
  234.0 9.8 %collective-permute-done.12 = f32[2,128,2,128]{3,1,2,0:T(8,128)} collective-permute-done((f32[2,128,2,128]{3,1,2,0:T(8,128)}, f32[2,128,2,128]{3,1,2,0:T(8,128)}, u32[]{:S(2)}, u32[]{:S(2)}) %collective-permute-start.12) | collective-permute-done | bytes 262176 | tf_op jit(solution)/shard_map/ppermute | solution.py:12
  243.8 10.8 %collective-permute-done.13 = f32[2,128,2,128]{3,1,2,0:T(8,128)} collective-permute-done((f32[2,128,2,128]{3,1,2,0:T(8,128)}, f32[2,128,2,128]{3,1,2,0:T(8,128)}, u32[]{:S(2)}, u32[]{:S(2)}) %collective-permute-start.13) | collective-permute-done | bytes 262176 | tf_op jit(solution)/shard_map/ppermute | solution.py:12
  254.6 12.0 %collective-permute-done.15 = f32[2,128,2,128]{3,1,2,0:T(8,128)} collective-permute-done((f32[2,128,2,128]{3,1,2,0:T(8,128)}, f32[2,128,2,128]{3,1,2,0:T(8,128)}, u32[]{:S(2)}, u32[]{:S(2)}) %collective-permute-start.15) | collective-permute-done | bytes 262176 | tf_op jit(solution)/shard_map/ppermute | solution.py:12
  266.6 11.9 %collective-permute-done.14 = f32[2,128,2,128]{3,1,2,0:T(8,128)} collective-permute-done((f32[2,128,2,128]{3,1,2,0:T(8,128)S(1)}, f32[2,128,2,128]{3,1,2,0:T(8,128)}, u32[]{:S(2)}, u32[]{:S(2)}) %collective-permute-start.14) | collective-permute-done | bytes 262176 | tf_op jit(solution)/shard_map/ppermute | solution.py:12
  283.3 366.5 %reduce-scatter.5.cloned.1.call-done = f32[1,84,512]{2,1,0:T(8,128)} async-done(((f32[64,84,512]{2,1,0:T(8,128)}), f32[1,84,512]{2,1,0:T(8,128)}) %reduce-scatter.5.cloned.1.call-update) | async-done | bytes 172048 | tf_op jit(solution)/shard_map/reduce_scatter | solution.py:75
  (71 shorter events, 43.4 us)
Async XLA Ops:
  7.2 57.9 %copy-start = (bf16[128,4,128]{2,1,0:T(4,128)(2,1)S(1)}, bf16[128,4,128]{2,1,0:T(4,128)(2,1)}, u32[]{:S(2)}) copy-start(bf16[128,4,128]{2,1,0:T(4,128)(2,1)} %param.6) | copy-start | bytes 393220
  7.2 141.5 %all-gather.6.cloned.1.call-start = ((), (), s32[]{:S(2)}) async-start(), calls=%async_computation.5 | async-start | bytes 5857280 | tf_op jit(solution)/shard_map/all_gather | solution.py:57
  7.9 165.7 %all-gather.4.cloned.1.call-start = ((), (), s32[]{:S(2)}) async-start(), calls=%async_computation.3 | async-start | bytes 1720320 | tf_op jit(solution)/shard_map/all_gather | solution.py:64
  8.9 56.1 %collective-permute-start.7 = (bf16[2,128,2,128]{3,1,2,0:T(8,128)(2,1)S(1)}, bf16[2,128,2,128]{3,1,2,0:T(8,128)(2,1)S(1)}, u32[]{:S(2)}, u32[]{:S(2)}) collective-permute-start(bf16[2,128,2,128]{3,1,2,0:T(8,128)(2,1)S(1)} %pad_maximum_fusion.1), channel_id=1, source_target_pairs={{0,4},{4,8},{8,12},{12,16},{16,20},{20,24},{24,28},{28,32},{32,36}... | collective-permute-start | bytes 393224 | tf_op jit(solution)/shard_map/ppermute | solution.py:12
  12.4 52.6 %collective-permute-start.6 = (bf16[2,128,2,128]{3,1,2,0:T(8,128)(2,1)S(1)}, bf16[2,128,2,128]{3,1,2,0:T(8,128)(2,1)S(1)}, u32[]{:S(2)}, u32[]{:S(2)}) collective-permute-start(bf16[2,128,2,128]{3,1,2,0:T(8,128)(2,1)S(1)} %pad_maximum_fusion.1), channel_id=1, source_target_pairs={{0,8},{4,12},{8,16},{12,20},{16,24},{20,28},{24,32},{28,36},{32,40... | collective-permute-start | bytes 393224 | tf_op jit(solution)/shard_map/ppermute | solution.py:12
  17.2 47.8 %collective-permute-start.5 = (bf16[2,128,2,128]{3,1,2,0:T(8,128)(2,1)S(1)}, bf16[2,128,2,128]{3,1,2,0:T(8,128)(2,1)S(1)}, u32[]{:S(2)}, u32[]{:S(2)}) collective-permute-start(bf16[2,128,2,128]{3,1,2,0:T(8,128)(2,1)S(1)} %pad_maximum_fusion.1), channel_id=1, source_target_pairs={{0,12},{4,16},{8,20},{12,24},{16,28},{20,32},{24,36},{28,40},{32,4... | collective-permute-start | bytes 393224 | tf_op jit(solution)/shard_map/ppermute | solution.py:12
  21.8 26.5 %collective-permute-start.1 = (bf16[2,128,2,128]{3,1,2,0:T(8,128)(2,1)S(1)}, bf16[2,128,2,128]{3,1,2,0:T(8,128)(2,1)S(1)}, u32[]{:S(2)}, u32[]{:S(2)}) collective-permute-start(bf16[2,128,2,128]{3,1,2,0:T(8,128)(2,1)S(1)} %pad_maximum_fusion.1), channel_id=1, source_target_pairs={{0,28},{4,32},{8,36},{12,40},{16,44},{20,48},{24,52},{28,56},{32,6... | collective-permute-start | bytes 393224 | tf_op jit(solution)/shard_map/ppermute | solution.py:12
  26.3 13.5 %collective-permute-start = (bf16[2,128,2,128]{3,1,2,0:T(8,128)(2,1)S(1)}, bf16[2,128,2,128]{3,1,2,0:T(8,128)(2,1)S(1)}, u32[]{:S(2)}, u32[]{:S(2)}) collective-permute-start(bf16[2,128,2,128]{3,1,2,0:T(8,128)(2,1)S(1)} %pad_maximum_fusion.1), channel_id=1, source_target_pairs={{0,32},{4,36},{8,40},{12,44},{16,48},{20,52},{24,56},{28,60},{32,6... | collective-permute-start | bytes 393224 | tf_op jit(solution)/shard_map/ppermute | solution.py:12
  31.8 249.6 %reduce-scatter.3.cloned.1.call-start = ((), (), s32[]{:S(2)}) async-start(), calls=%async_computation.2 | async-start | bytes 3440640 | tf_op jit(solution)/shard_map/reduce_scatter | solution.py:61
  39.7 14.7 %collective-permute-start.2 = (bf16[2,128,2,128]{3,1,2,0:T(8,128)(2,1)S(1)}, bf16[2,128,2,128]{3,1,2,0:T(8,128)(2,1)S(1)}, u32[]{:S(2)}, u32[]{:S(2)}) collective-permute-start(bf16[2,128,2,128]{3,1,2,0:T(8,128)(2,1)S(1)} %pad_maximum_fusion.1), channel_id=1, source_target_pairs={{0,24},{4,28},{8,32},{12,36},{16,40},{20,44},{24,48},{28,52},{32,5... | collective-permute-start | bytes 393224 | tf_op jit(solution)/shard_map/ppermute | solution.py:12
  48.3 15.4 %collective-permute-start.3 = (bf16[2,128,2,128]{3,1,2,0:T(8,128)(2,1)S(1)}, bf16[2,128,2,128]{3,1,2,0:T(8,128)(2,1)S(1)}, u32[]{:S(2)}, u32[]{:S(2)}) collective-permute-start(bf16[2,128,2,128]{3,1,2,0:T(8,128)(2,1)S(1)} %pad_maximum_fusion.1), channel_id=1, source_target_pairs={{0,20},{4,24},{8,28},{12,32},{16,36},{20,40},{24,44},{28,48},{32,5... | collective-permute-start | bytes 393224 | tf_op jit(solution)/shard_map/ppermute | solution.py:12
  54.5 10.5 %collective-permute-start.4 = (bf16[2,128,2,128]{3,1,2,0:T(8,128)(2,1)S(1)}, bf16[2,128,2,128]{3,1,2,0:T(8,128)(2,1)S(1)}, u32[]{:S(2)}, u32[]{:S(2)}) collective-permute-start(bf16[2,128,2,128]{3,1,2,0:T(8,128)(2,1)S(1)} %pad_maximum_fusion.1), channel_id=1, source_target_pairs={{0,16},{4,20},{8,24},{12,28},{16,32},{20,36},{24,40},{28,44},{32,4... | collective-permute-start | bytes 393224 | tf_op jit(solution)/shard_map/ppermute | solution.py:12
  65.1 112.5 %copy-start.3 = (bf16[2,1152,2,128]{3,1,2,0:T(8,128)(2,1)}, bf16[2,1152,2,128]{3,1,2,0:T(8,128)(2,1)S(1)}, u32[]{:S(2)}) copy-start(bf16[2,1152,2,128]{3,1,2,0:T(8,128)(2,1)S(1)} %constant_dynamic-update-slice_fusion) | copy-start | bytes 3538948
  183.8 466.0 %reduce-scatter.5.cloned.1.call-start = ((), (), s32[]{:S(2)}) async-start(), calls=%async_computation.4 | async-start | bytes 11714560 | tf_op jit(solution)/shard_map/reduce_scatter | solution.py:75
  196.5 36.4 %copy-start.5 = (bf16[2,1152,2,128]{3,1,2,0:T(8,128)(2,1)S(1)}, bf16[2,1152,2,128]{3,1,2,0:T(8,128)(2,1)}, u32[]{:S(2)}) copy-start(bf16[2,1152,2,128]{3,1,2,0:T(8,128)(2,1)} %copy-done.3) | copy-start | bytes 3538948
  197.8 80.7 %copy-start.2 = (f32[1,1152,2,128]{3,1,2,0:T(8,128)S(1)}, f32[1,1152,2,128]{3,1,2,0:T(8,128)}, u32[]{:S(2)}) copy-start(f32[1,1152,2,128]{3,1,2,0:T(8,128)} %copy-done.1) | copy-start | bytes 3538948
  197.8 23.0 %collective-permute-start.8 = (f32[2,128,2,128]{3,1,2,0:T(8,128)S(1)}, f32[2,128,2,128]{3,1,2,0:T(8,128)S(1)}, u32[]{:S(2)}, u32[]{:S(2)}) collective-permute-start(f32[2,128,2,128]{3,1,2,0:T(8,128)S(1)} %get-tuple-element.20), channel_id=1, source_target_pairs={{4,0},{8,4},{12,8},{16,12},{20,16},{24,20},{28,24},{32,28},{36,32}... | collective-permute-start | bytes 786440 | tf_op jit(solution)/shard_map/ppermute | solution.py:12
  206.1 18.0 %collective-permute-start.9 = (f32[2,128,2,128]{3,1,2,0:T(8,128)S(1)}, f32[2,128,2,128]{3,1,2,0:T(8,128)S(1)}, u32[]{:S(2)}, u32[]{:S(2)}) collective-permute-start(f32[2,128,2,128]{3,1,2,0:T(8,128)S(1)} %get-tuple-element.21), channel_id=1, source_target_pairs={{8,0},{12,4},{16,8},{20,12},{24,16},{28,20},{32,24},{36,28},{40,32... | collective-permute-start | bytes 786440 | tf_op jit(solution)/shard_map/ppermute | solution.py:12
  208.9 18.6 %collective-permute-start.10 = (f32[2,128,2,128]{3,1,2,0:T(8,128)S(1)}, f32[2,128,2,128]{3,1,2,0:T(8,128)S(1)}, u32[]{:S(2)}, u32[]{:S(2)}) collective-permute-start(f32[2,128,2,128]{3,1,2,0:T(8,128)S(1)} %get-tuple-element.22), channel_id=1, source_target_pairs={{12,0},{16,4},{20,8},{24,12},{28,16},{32,20},{36,24},{40,28},{44,3... | collective-permute-start | bytes 786440 | tf_op jit(solution)/shard_map/ppermute | solution.py:12
  212.5 21.5 %collective-permute-start.11 = (f32[2,128,2,128]{3,1,2,0:T(8,128)}, f32[2,128,2,128]{3,1,2,0:T(8,128)}, u32[]{:S(2)}, u32[]{:S(2)}) collective-permute-start(f32[2,128,2,128]{3,1,2,0:T(8,128)} %get-tuple-element.23), channel_id=1, source_target_pairs={{16,0},{20,4},{24,8},{28,12},{32,16},{36,20},{40,24},{44,28},{48,3... | collective-permute-start | bytes 786440 | tf_op jit(solution)/shard_map/ppermute | solution.py:12
  215.8 28.0 %collective-permute-start.12 = (f32[2,128,2,128]{3,1,2,0:T(8,128)}, f32[2,128,2,128]{3,1,2,0:T(8,128)}, u32[]{:S(2)}, u32[]{:S(2)}) collective-permute-start(f32[2,128,2,128]{3,1,2,0:T(8,128)} %get-tuple-element.24), channel_id=1, source_target_pairs={{20,0},{24,4},{28,8},{32,12},{36,16},{40,20},{44,24},{48,28},{52,3... | collective-permute-start | bytes 786440 | tf_op jit(solution)/shard_map/ppermute | solution.py:12
  220.9 33.8 %collective-permute-start.13 = (f32[2,128,2,128]{3,1,2,0:T(8,128)}, f32[2,128,2,128]{3,1,2,0:T(8,128)}, u32[]{:S(2)}, u32[]{:S(2)}) collective-permute-start(f32[2,128,2,128]{3,1,2,0:T(8,128)} %get-tuple-element.25), channel_id=1, source_target_pairs={{24,0},{28,4},{32,8},{36,12},{40,16},{44,20},{48,24},{52,28},{56,3... | collective-permute-start | bytes 786440 | tf_op jit(solution)/shard_map/ppermute | solution.py:12
  224.1 42.5 %collective-permute-start.15 = (f32[2,128,2,128]{3,1,2,0:T(8,128)}, f32[2,128,2,128]{3,1,2,0:T(8,128)}, u32[]{:S(2)}, u32[]{:S(2)}) collective-permute-start(f32[2,128,2,128]{3,1,2,0:T(8,128)} %get-tuple-element.26), channel_id=1, source_target_pairs={{32,0},{36,4},{40,8},{44,12},{48,16},{52,20},{56,24},{60,28},{64,3... | collective-permute-start | bytes 786440 | tf_op jit(solution)/shard_map/ppermute | solution.py:12
  227.5 51.1 %collective-permute-start.14 = (f32[2,128,2,128]{3,1,2,0:T(8,128)S(1)}, f32[2,128,2,128]{3,1,2,0:T(8,128)}, u32[]{:S(2)}, u32[]{:S(2)}) collective-permute-start(f32[2,128,2,128]{3,1,2,0:T(8,128)S(1)} %get-tuple-element.27), channel_id=1, source_target_pairs={{28,0},{32,4},{36,8},{40,12},{44,16},{48,20},{52,24},{56,28},{60,3... | collective-permute-start | bytes 786440 | tf_op jit(solution)/shard_map/ppermute | solution.py:12
  (3 other events, 8.4 us)
Sparse Core Ops, SparseCore 0:
  11.6 137.0 all-gather.5
  150.5 23.0 all-gather.3
  183.9 37.0 reduce-scatter.2
  223.5 426.2 reduce-scatter.4
where the time goes:
time: 659 us; the launch traced here: 658 us
  waiting for transfers between devices  521 us (79%)
  starting transfers between devices  74.7 us (11%)
  matrix products  22 us (3%)
  local copies, waits for them, and re-layouts  16.8 us (3%)
  between operations  14.2 us (2%)
  other arithmetic  9.75 us (1%)
    reduce_scatter x1, waiting for transfers between devices, shards(): lax.psum_scatter(proj_partial, 'ctx', scatter_dimension=0, tiled=True)  367 us
    all_gather x1, waiting for transfers between devices, shards(): proj_full = lax.all_gather(out_proj, 'ctx', axis=0, tiled=True)  79.3 us
    ppermute x16, starting transfers between devices, passed_along(): return lax.ppermute(value, axis, pairs)  74.5 us
    ppermute x16, waiting for transfers between devices, passed_along(): return lax.ppermute(value, axis, pairs)  58.1 us
    all_gather x1, waiting for transfers between devices, shards(): grad_full = lax.all_gather(out_grad, 'head', axis=1, tiled=True)  16 us
  transfers between devices with their start and end apart: 20, of which 11 were waited for; matrix products, arithmetic and copies ran while one was open for 5% of the time, Pallas kernels for 0%

commit v1 on v0

--- a/solution.py
+++ b/solution.py
@@ -61,7 +61,9 @@
     layer_out = lax.psum_scatter(out_partial, "head", scatter_dimension=1, tiled=True).astype(
         jnp.bfloat16
     )
-    grad_full = lax.all_gather(out_grad, "head", axis=1, tiled=True)
+    grad_full = jnp.concatenate(
+        lax.all_to_all(jnp.stack([out_grad] * lax.axis_size("head")), "head", 0, 0), axis=1
+    )
     grad_attended = jnp.dot(grad_full, proj_full, preferred_element_type=jnp.float32).astype(
         jnp.bfloat16
     )

time: 659 us -> 648 us (0.983)
  waiting for transfers between devices: 521 us -> 503 us
    all_gather x1 -> x0, waiting for transfers between devices: 16 us -> none  [shards(): grad_full = lax.all_gather(out_grad, 'head', axis=1, tiled=True)]
    ppermute x16, waiting for transfers between devices: 58.1 us -> 46.1 us  [passed_along(): return lax.ppermute(value, axis, pairs)]
    reduce_scatter x1, waiting for transfers between devices: 367 us -> 377 us  [shards(): lax.psum_scatter(proj_partial, 'ctx', scatter_dimension=0, tiled=True)]
    unnamed x26 -> x30, local copies, waits for them, and re-layouts: 12.7 us -> 15.5 us
  transfers between devices with their start and end apart: 20 -> 20, of which waited for: 11 -> 9; matrix products, arithmetic and copies ran while one was open for 5% -> 6% of each run, Pallas kernels for 0% -> 0%
where the time goes in v1:
time: 648 us; the launch traced here: 646 us
  waiting for transfers between devices  503 us (78%)
  starting transfers between devices  75.7 us (12%)
  matrix products  24 us (4%)
  local copies, waits for them, and re-layouts  20.1 us (3%)
  between operations  14.2 us (2%)
  other arithmetic  9.06 us (1%)
    reduce_scatter x1, waiting for transfers between devices, shards(): lax.psum_scatter(proj_partial, 'ctx', scatter_dimension=0, tiled=True)  377 us
    all_gather x1, waiting for transfers between devices, shards(): proj_full = lax.all_gather(out_proj, 'ctx', axis=0, tiled=True)  78.7 us
    ppermute x16, starting transfers between devices, passed_along(): return lax.ppermute(value, axis, pairs)  71.2 us
    ppermute x16, waiting for transfers between devices, passed_along(): return lax.ppermute(value, axis, pairs)  46.1 us
    unnamed x30, local copies, waits for them, and re-layouts  15.5 us
  transfers between devices with their start and end apart: 20, of which 9 were waited for; matrix products, arithmetic and copies ran while one was open for 6% of the time, Pallas kernels for 0%

profile of v1, /device:TPU:6, one launch (start us, length us, event | category | flops | bytes accessed | tf_op | source)
XLA Modules:
  0.0 645.9 jit_solution(14024646602604563679)
XLA Ops:
  8.8 3.5 collective-permute-start.7
  12.3 4.8 collective-permute-start.6
  17.1 4.6 collective-permute-start.5
  21.8 4.5 collective-permute-start.1
  26.2 5.5 collective-permute-start
  34.0 4.5 all-to-all-start
  40.4 8.5 %collective-permute-start.2 = (bf16[2,128,2,128]{3,1,2,0:T(8,128)(2,1)S(1)}, bf16[2,128,2,128]{3,1,2,0:T(8,128)(2,1)S(1)}, u32[]{:S(2)}, u32[]{:S(2)}) collective-permute-start(bf16[2,128,2,128]{3,1,2,0:T(8,128)(2,1)S(1)} %pad_maximum_fusion.1), channel_id=1, source_target_pairs={{0,24},{4,28},{8,32},{12,36},{16,40},{20,44},{24,48},{28,52},{32,5... | collective-permute-start | bytes 393224 | tf_op jit(solution)/shard_map/ppermute | solution.py:12
  55.6 6.9 %collective-permute-start.4 = (bf16[2,128,2,128]{3,1,2,0:T(8,128)(2,1)S(1)}, bf16[2,128,2,128]{3,1,2,0:T(8,128)(2,1)S(1)}, u32[]{:S(2)}, u32[]{:S(2)}) collective-permute-start(bf16[2,128,2,128]{3,1,2,0:T(8,128)(2,1)S(1)} %pad_maximum_fusion.1), channel_id=1, source_target_pairs={{0,16},{4,20},{8,24},{12,28},{16,32},{20,36},{24,40},{28,44},{32,4... | collective-permute-start | bytes 393224 | tf_op jit(solution)/shard_map/ppermute | solution.py:12
  62.5 4.1 collective-permute-done.3
  71.1 78.7 %all-gather.3.cloned.1.call-done = bf16[64,84,512]{2,1,0:T(8,128)(2,1)} async-done(((bf16[1,84,512]{2,1,0:T(8,128)(2,1)}), bf16[64,84,512]{2,1,0:T(8,128)(2,1)}) %all-gather.3.cloned.1.call-update) | async-done | bytes 5505040 | tf_op jit(solution)/shard_map/all_gather | solution.py:57
  149.8 8.9 %reshape.59 = bf16[5376,512]{1,0:T(8,128)(2,1)} reshape(bf16[64,84,512]{2,1,0:T(8,128)(2,1)} %all-gather.3.cloned.1.call-done) | data formatting | bytes 11010048
  158.7 3.5 convolution_convert_fusion
  163.7 5.8 fusion.45
  170.8 7.4 %convolution_bitcast_fusion = f32[64,84,512]{2,1,0:T(8,128)} fusion(bf16[128,512,1]{0,1,2:T(8,128)(2,1)S(1)} %bitcast.113, bf16[128,64,84]{0,2,1:T(8,128)(2,1)} %reshape_reshape.3), kind=kOutput, calls=%fused_computation.17 | convolution fusion | flops 704643072 | bytes 12517376 | tf_op jit(solution)/shard_map/tcr,tj->crj/dot_general | solution.py:71
  184.2 7.5 %collective-permute-start.8 = (f32[2,128,2,128]{3,1,2,0:T(8,128)S(1)}, f32[2,128,2,128]{3,1,2,0:T(8,128)S(1)}, u32[]{:S(2)}, u32[]{:S(2)}) collective-permute-start(f32[2,128,2,128]{3,1,2,0:T(8,128)S(1)} %get-tuple-element.20), channel_id=1, source_target_pairs={{4,0},{8,4},{12,8},{16,12},{20,16},{24,20},{28,24},{32,28},{36,32}... | collective-permute-start | bytes 786440 | tf_op jit(solution)/shard_map/ppermute | solution.py:12
  197.5 3.2 collective-permute-start.11
  200.7 4.1 collective-permute-start.12
  204.8 5.0 collective-permute-start.13
  209.8 3.6 collective-permute-start.15
  216.5 21.2 %collective-permute-done.11 = f32[2,128,2,128]{3,1,2,0:T(8,128)} collective-permute-done((f32[2,128,2,128]{3,1,2,0:T(8,128)}, f32[2,128,2,128]{3,1,2,0:T(8,128)}, u32[]{:S(2)}, u32[]{:S(2)}) %collective-permute-start.11) | collective-permute-done | bytes 262176 | tf_op jit(solution)/shard_map/ppermute | solution.py:12
  237.7 5.8 collective-permute-done.12
  243.4 5.6 collective-permute-done.13
  249.1 3.8 collective-permute-done.15
  260.3 377.5 %reduce-scatter.5.cloned.1.call-done = f32[1,84,512]{2,1,0:T(8,128)} async-done(((f32[64,84,512]{2,1,0:T(8,128)}), f32[1,84,512]{2,1,0:T(8,128)}) %reduce-scatter.5.cloned.1.call-update) | async-done | bytes 172048 | tf_op jit(solution)/shard_map/reduce_scatter | solution.py:77
  (75 shorter events, 43.6 us)
Async XLA Ops:
  7.2 59.6 %copy-start = (bf16[128,4,128]{2,1,0:T(4,128)(2,1)S(1)}, bf16[128,4,128]{2,1,0:T(4,128)(2,1)}, u32[]{:S(2)}) copy-start(bf16[128,4,128]{2,1,0:T(4,128)(2,1)} %param.6) | copy-start | bytes 393220
  7.2 142.6 %all-gather.3.cloned.1.call-start = ((), (), s32[]{:S(2)}) async-start(), calls=%async_computation.5 | async-start | bytes 5857280 | tf_op jit(solution)/shard_map/all_gather | solution.py:57
  8.8 57.9 %collective-permute-start.7 = (bf16[2,128,2,128]{3,1,2,0:T(8,128)(2,1)S(1)}, bf16[2,128,2,128]{3,1,2,0:T(8,128)(2,1)S(1)}, u32[]{:S(2)}, u32[]{:S(2)}) collective-permute-start(bf16[2,128,2,128]{3,1,2,0:T(8,128)(2,1)S(1)} %pad_maximum_fusion.1), channel_id=1, source_target_pairs={{0,4},{4,8},{8,12},{12,16},{16,20},{20,24},{24,28},{28,32},{32,36}... | collective-permute-start | bytes 393224 | tf_op jit(solution)/shard_map/ppermute | solution.py:12
  12.3 54.4 %collective-permute-start.6 = (bf16[2,128,2,128]{3,1,2,0:T(8,128)(2,1)S(1)}, bf16[2,128,2,128]{3,1,2,0:T(8,128)(2,1)S(1)}, u32[]{:S(2)}, u32[]{:S(2)}) collective-permute-start(bf16[2,128,2,128]{3,1,2,0:T(8,128)(2,1)S(1)} %pad_maximum_fusion.1), channel_id=1, source_target_pairs={{0,8},{4,12},{8,16},{12,20},{16,24},{20,28},{24,32},{28,36},{32,40... | collective-permute-start | bytes 393224 | tf_op jit(solution)/shard_map/ppermute | solution.py:12
  17.1 49.5 %collective-permute-start.5 = (bf16[2,128,2,128]{3,1,2,0:T(8,128)(2,1)S(1)}, bf16[2,128,2,128]{3,1,2,0:T(8,128)(2,1)S(1)}, u32[]{:S(2)}, u32[]{:S(2)}) collective-permute-start(bf16[2,128,2,128]{3,1,2,0:T(8,128)(2,1)S(1)} %pad_maximum_fusion.1), channel_id=1, source_target_pairs={{0,12},{4,16},{8,20},{12,24},{16,28},{20,32},{24,36},{28,40},{32,4... | collective-permute-start | bytes 393224 | tf_op jit(solution)/shard_map/ppermute | solution.py:12
  21.8 28.1 %collective-permute-start.1 = (bf16[2,128,2,128]{3,1,2,0:T(8,128)(2,1)S(1)}, bf16[2,128,2,128]{3,1,2,0:T(8,128)(2,1)}, u32[]{:S(2)}, u32[]{:S(2)}) collective-permute-start(bf16[2,128,2,128]{3,1,2,0:T(8,128)(2,1)S(1)} %pad_maximum_fusion.1), channel_id=1, source_target_pairs={{0,28},{4,32},{8,36},{12,40},{16,44},{20,48},{24,52},{28,56},{32,6... | collective-permute-start | bytes 393224 | tf_op jit(solution)/shard_map/ppermute | solution.py:12
  26.2 13.5 %collective-permute-start = (bf16[2,128,2,128]{3,1,2,0:T(8,128)(2,1)S(1)}, bf16[2,128,2,128]{3,1,2,0:T(8,128)(2,1)S(1)}, u32[]{:S(2)}, u32[]{:S(2)}) collective-permute-start(bf16[2,128,2,128]{3,1,2,0:T(8,128)(2,1)S(1)} %pad_maximum_fusion.1), channel_id=1, source_target_pairs={{0,32},{4,36},{8,40},{12,44},{16,48},{20,52},{24,56},{28,60},{32,6... | collective-permute-start | bytes 393224 | tf_op jit(solution)/shard_map/ppermute | solution.py:12
  34.0 4.5 copy-start.8
  34.0 124.7 %all-to-all-start = ((bf16[4,128,1344]{1,2,0:T(8,128)(2,1)}), bf16[4,128,1344]{1,2,0:T(8,128)(2,1)S(1)}, u32[]{:S(2)}, u32[]{:S(2)}) async-start(bf16[4,128,1344]{1,2,0:T(8,128)(2,1)} %stack.28), calls=%async_computation.1 | async-start | bytes 2752512 | tf_op jit(solution)/shard_map/all_to_all | solution.py:65
  38.5 219.9 %reduce-scatter.3.cloned.1.call-start = ((), (), s32[]{:S(2)}) async-start(), calls=%async_computation.3 | async-start | bytes 3440640 | tf_op jit(solution)/shard_map/reduce_scatter | solution.py:61
  40.4 15.2 %collective-permute-start.2 = (bf16[2,128,2,128]{3,1,2,0:T(8,128)(2,1)S(1)}, bf16[2,128,2,128]{3,1,2,0:T(8,128)(2,1)S(1)}, u32[]{:S(2)}, u32[]{:S(2)}) collective-permute-start(bf16[2,128,2,128]{3,1,2,0:T(8,128)(2,1)S(1)} %pad_maximum_fusion.1), channel_id=1, source_target_pairs={{0,24},{4,28},{8,32},{12,36},{16,40},{20,44},{24,48},{28,52},{32,5... | collective-permute-start | bytes 393224 | tf_op jit(solution)/shard_map/ppermute | solution.py:12
  49.8 16.8 %collective-permute-start.3 = (bf16[2,128,2,128]{3,1,2,0:T(8,128)(2,1)S(1)}, bf16[2,128,2,128]{3,1,2,0:T(8,128)(2,1)S(1)}, u32[]{:S(2)}, u32[]{:S(2)}) collective-permute-start(bf16[2,128,2,128]{3,1,2,0:T(8,128)(2,1)S(1)} %pad_maximum_fusion.1), channel_id=1, source_target_pairs={{0,20},{4,24},{8,28},{12,32},{16,36},{20,40},{24,44},{28,48},{32,5... | collective-permute-start | bytes 393224 | tf_op jit(solution)/shard_map/ppermute | solution.py:12
  55.6 11.0 %collective-permute-start.4 = (bf16[2,128,2,128]{3,1,2,0:T(8,128)(2,1)S(1)}, bf16[2,128,2,128]{3,1,2,0:T(8,128)(2,1)S(1)}, u32[]{:S(2)}, u32[]{:S(2)}) collective-permute-start(bf16[2,128,2,128]{3,1,2,0:T(8,128)(2,1)S(1)} %pad_maximum_fusion.1), channel_id=1, source_target_pairs={{0,16},{4,20},{8,24},{12,28},{16,32},{20,36},{24,40},{28,44},{32,4... | collective-permute-start | bytes 393224 | tf_op jit(solution)/shard_map/ppermute | solution.py:12
  169.5 468.3 %reduce-scatter.5.cloned.1.call-start = ((), (), s32[]{:S(2)}) async-start(), calls=%async_computation.4 | async-start | bytes 11714560 | tf_op jit(solution)/shard_map/reduce_scatter | solution.py:77
  182.8 32.5 %copy-start.5 = (bf16[2,1152,2,128]{3,1,2,0:T(8,128)(2,1)S(1)}, bf16[2,1152,2,128]{3,1,2,0:T(8,128)(2,1)}, u32[]{:S(2)}) copy-start(bf16[2,1152,2,128]{3,1,2,0:T(8,128)(2,1)} %copy-done.3) | copy-start | bytes 3538948
  184.2 71.4 %copy-start.2 = (f32[1,1152,2,128]{3,1,2,0:T(8,128)S(1)}, f32[1,1152,2,128]{3,1,2,0:T(8,128)}, u32[]{:S(2)}) copy-start(f32[1,1152,2,128]{3,1,2,0:T(8,128)} %copy-done.1) | copy-start | bytes 3538948
  184.2 20.6 %collective-permute-start.8 = (f32[2,128,2,128]{3,1,2,0:T(8,128)S(1)}, f32[2,128,2,128]{3,1,2,0:T(8,128)S(1)}, u32[]{:S(2)}, u32[]{:S(2)}) collective-permute-start(f32[2,128,2,128]{3,1,2,0:T(8,128)S(1)} %get-tuple-element.20), channel_id=1, source_target_pairs={{4,0},{8,4},{12,8},{16,12},{20,16},{24,20},{28,24},{32,28},{36,32}... | collective-permute-start | bytes 786440 | tf_op jit(solution)/shard_map/ppermute | solution.py:12
  191.7 18.1 %collective-permute-start.9 = (f32[2,128,2,128]{3,1,2,0:T(8,128)S(1)}, f32[2,128,2,128]{3,1,2,0:T(8,128)S(1)}, u32[]{:S(2)}, u32[]{:S(2)}) collective-permute-start(f32[2,128,2,128]{3,1,2,0:T(8,128)S(1)} %get-tuple-element.21), channel_id=1, source_target_pairs={{8,0},{12,4},{16,8},{20,12},{24,16},{28,20},{32,24},{36,28},{40,32... | collective-permute-start | bytes 786440 | tf_op jit(solution)/shard_map/ppermute | solution.py:12
  194.4 18.9 %collective-permute-start.10 = (f32[2,128,2,128]{3,1,2,0:T(8,128)S(1)}, f32[2,128,2,128]{3,1,2,0:T(8,128)S(1)}, u32[]{:S(2)}, u32[]{:S(2)}) collective-permute-start(f32[2,128,2,128]{3,1,2,0:T(8,128)S(1)} %get-tuple-element.22), channel_id=1, source_target_pairs={{12,0},{16,4},{20,8},{24,12},{28,16},{32,20},{36,24},{40,28},{44,3... | collective-permute-start | bytes 786440 | tf_op jit(solution)/shard_map/ppermute | solution.py:12
  197.5 40.2 %collective-permute-start.11 = (f32[2,128,2,128]{3,1,2,0:T(8,128)}, f32[2,128,2,128]{3,1,2,0:T(8,128)}, u32[]{:S(2)}, u32[]{:S(2)}) collective-permute-start(f32[2,128,2,128]{3,1,2,0:T(8,128)} %get-tuple-element.23), channel_id=1, source_target_pairs={{16,0},{20,4},{24,8},{28,12},{32,16},{36,20},{40,24},{44,28},{48,3... | collective-permute-start | bytes 786440 | tf_op jit(solution)/shard_map/ppermute | solution.py:12
  200.7 42.8 %collective-permute-start.12 = (f32[2,128,2,128]{3,1,2,0:T(8,128)}, f32[2,128,2,128]{3,1,2,0:T(8,128)}, u32[]{:S(2)}, u32[]{:S(2)}) collective-permute-start(f32[2,128,2,128]{3,1,2,0:T(8,128)} %get-tuple-element.24), channel_id=1, source_target_pairs={{20,0},{24,4},{28,8},{32,12},{36,16},{40,20},{44,24},{48,28},{52,3... | collective-permute-start | bytes 786440 | tf_op jit(solution)/shard_map/ppermute | solution.py:12
  204.8 44.3 %collective-permute-start.13 = (f32[2,128,2,128]{3,1,2,0:T(8,128)}, f32[2,128,2,128]{3,1,2,0:T(8,128)}, u32[]{:S(2)}, u32[]{:S(2)}) collective-permute-start(f32[2,128,2,128]{3,1,2,0:T(8,128)} %get-tuple-element.25), channel_id=1, source_target_pairs={{24,0},{28,4},{32,8},{36,12},{40,16},{44,20},{48,24},{52,28},{56,3... | collective-permute-start | bytes 786440 | tf_op jit(solution)/shard_map/ppermute | solution.py:12
  209.8 43.1 %collective-permute-start.15 = (f32[2,128,2,128]{3,1,2,0:T(8,128)}, f32[2,128,2,128]{3,1,2,0:T(8,128)}, u32[]{:S(2)}, u32[]{:S(2)}) collective-permute-start(f32[2,128,2,128]{3,1,2,0:T(8,128)} %get-tuple-element.26), channel_id=1, source_target_pairs={{32,0},{36,4},{40,8},{44,12},{48,16},{52,20},{56,24},{60,28},{64,3... | collective-permute-start | bytes 786440 | tf_op jit(solution)/shard_map/ppermute | solution.py:12
  213.4 42.2 %collective-permute-start.14 = (f32[2,128,2,128]{3,1,2,0:T(8,128)S(1)}, f32[2,128,2,128]{3,1,2,0:T(8,128)}, u32[]{:S(2)}, u32[]{:S(2)}) collective-permute-start(f32[2,128,2,128]{3,1,2,0:T(8,128)S(1)} %get-tuple-element.27), channel_id=1, source_target_pairs={{28,0},{32,4},{36,8},{40,12},{44,16},{48,20},{52,24},{56,28},{60,3... | collective-permute-start | bytes 786440 | tf_op jit(solution)/shard_map/ppermute | solution.py:12
  (5 other events, 8.3 us)
Sparse Core Ops, SparseCore 0:
  11.6 138.1 all-gather.2
  169.6 33.5 reduce-scatter.2
  205.8 431.9 reduce-scatter.4
